TPU v7x, 32 devices: a whole 2x2x4 slice. The times are simulated.
32 devices in a mesh: groups: 2 (over x), seq: 16 (over z, y, core).
Axes of the slice: x: 2, y: 2, z: 4, core: 2. Of those that a mesh axis runs over, the one named last changes fastest.
Arguments:
- video_q: bfloat16 [16384, 2048], P(('groups', 'seq')), parts along dimension 0, may hold values from -64 to 64
- video_k: bfloat16 [16384, 2048], P(('groups', 'seq')), parts along dimension 0, may hold values from -6 to 6
- video_v: bfloat16 [16384, 2048], P(('groups', 'seq')), parts along dimension 0, may hold values from -4 to 4
- audio_q: bfloat16 [256, 2048], P(('groups', 'seq')), parts along dimension 0, may hold values from -64 to 64
- audio_k: bfloat16 [256, 2048], P(('groups', 'seq')), parts along dimension 0, may hold values from -6 to 6
- audio_v: bfloat16 [256, 2048], P(('groups', 'seq')), parts along dimension 0, may hold values from -4 to 4
Outputs:
- video_out: bfloat16 [16384, 2048], P(('groups', 'seq')), parts along dimension 0
- audio_out: bfloat16 [256, 2048], P(('groups', 'seq')), parts along dimension 0
There are 2 independent parts, one for each index of `groups`. A program takes and returns all parts, laid end to end along the dimension named above; each array names one. Nothing has to cross between parts.
All inputs are finite; a program needn't handle non-finite values.
Results may differ from a plain program's by a relative error of at most 0.007.
Values may be sent and summed in bfloat16 or wider, within the bound.
No kernel may reach another device: no remote copies, remote signals or barrier semaphores. Data moves between devices by JAX's collectives and lax.ppermute only.
A program may use at most 128 MiB of HBM per device.

v0:
```python
import math
import jax
import jax.numpy as jnp
from jax import lax
from jax.sharding import PartitionSpec as P

lowest_score = -1e30


def spread(scales):
    return jnp.repeat(scales, 64, axis=1)


def partial_block(queries, keys, values):
    head_count = queries.shape[1] // 64
    query_heads = queries.reshape(queries.shape[0], head_count, 64)
    key_heads = keys.reshape(keys.shape[0], head_count, 64)
    value_heads = values.reshape(values.shape[0], head_count, 64)
    scores = (
        jnp.einsum("rhd,shd->hrs", query_heads, key_heads, preferred_element_type=jnp.float32)
        * 0.125
    )
    highest = jnp.max(scores, axis=2)
    weights = jnp.exp(scores - highest[:, :, None])
    totals = jnp.sum(weights, axis=2)
    summed = jnp.einsum(
        "hrs,shd->rhd",
        weights.astype(jnp.bfloat16),
        value_heads,
        preferred_element_type=jnp.float32,
    )
    return (highest.T, totals.T, summed.reshape(queries.shape[0], head_count * 64))


def combine(earlier, later):
    highest = jnp.maximum(earlier[0], later[0])
    earlier_scale = jnp.exp(earlier[0] - highest)
    later_scale = jnp.exp(later[0] - highest)
    totals = earlier[1] * earlier_scale + later[1] * later_scale
    summed = earlier[2] * spread(earlier_scale) + later[2] * spread(later_scale)
    return (highest, totals, summed)


def blocked_partial(queries, keys, values):
    row_count = queries.shape[0]
    model_width = queries.shape[1]
    block_rows = math.gcd(row_count, 128)
    stacked = queries.reshape(row_count // block_rows, block_rows, model_width)
    newest = lax.map(lambda query_rows: partial_block(query_rows, keys, values), stacked)
    return tuple((member.reshape(row_count, member.shape[2]) for member in newest))


def empty_state(row_count, model_width):
    head_count = model_width // 64
    return (
        jnp.full((row_count, head_count), lowest_score, jnp.float32),
        jnp.zeros((row_count, head_count), jnp.float32),
        jnp.zeros((row_count, model_width), jnp.float32),
    )


def local(video_q, video_k, video_v, audio_q, audio_k, audio_v):
    tok_rows = video_q.shape[0]
    model_width = video_q.shape[1]
    pieces = (
        lax.all_gather(audio_k, "seq", axis=0, tiled=True),
        lax.all_gather(audio_v, "seq", axis=0, tiled=True),
    )
    newest = blocked_partial(video_q, pieces[0], pieces[1])
    highest, totals, summed = combine(empty_state(tok_rows, model_width), newest)
    video_out = (summed / spread(totals)).astype(jnp.bfloat16)
    key_heads, value_heads, query_heads = (
        lax.all_to_all(video_k, "seq", split_axis=1, concat_axis=0, tiled=True),
        lax.all_to_all(video_v, "seq", split_axis=1, concat_axis=0, tiled=True),
        lax.all_to_all(audio_q, "seq", split_axis=1, concat_axis=0, tiled=True),
    )
    total_keys = key_heads.shape[0]
    columns = key_heads.shape[1]
    key_block = math.gcd(total_keys, 4096)
    block_count = total_keys // key_block

    def advance(running, pieces):
        return (combine(running, partial_block(query_heads, pieces[0], pieces[1])), None)

    state, ignored = lax.scan(
        advance,
        empty_state(query_heads.shape[0], columns),
        (
            key_heads.reshape(block_count, key_block, columns),
            value_heads.reshape(block_count, key_block, columns),
        ),
    )
    head_out = (state[2] / spread(state[1])).astype(jnp.bfloat16)
    audio_out = lax.all_to_all(head_out, "seq", split_axis=0, concat_axis=1, tiled=True)
    return (video_out, audio_out)


def solution(mesh):
    placed = (
        P(("groups", "seq"), None),
        P(("groups", "seq"), None),
        P(("groups", "seq"), None),
        P(("groups", "seq"), None),
        P(("groups", "seq"), None),
        P(("groups", "seq"), None),
    )
    return jax.shard_map(
        local,
        mesh=mesh,
        in_specs=placed,
        out_specs=(P(("groups", "seq"), None), P(("groups", "seq"), None)),
        check_vma=False,
    )
```

profile of v0, /device:TPU:0, one launch (start us, length us, event | category | flops | bytes accessed | tf_op | source)
XLA Modules:
  0.0 264.3 jit_solution(13597468701080333482)
XLA Ops:
  0.6 7.4 %all-to-all-start.1 = ((bf16[8,16,128]{2,0,1:T(8,128)(2,1)}), bf16[8,16,128]{2,0,1:T(8,128)(2,1)S(1)}, u32[]{:S(2)}, u32[]{:S(2)}) async-start(bf16[8,16,128]{2,0,1:T(8,128)(2,1)} %bitcast.158), calls=%async_computation.1 | async-start | bytes 65536 | tf_op jit(solution)/shard_map/all_to_all | solution.py:75
  8.0 3.9 %copy.57 = bf16[512,2048]{0,1:T(8,128)(2,1)} copy(bf16[512,2048]{1,0:T(8,128)(2,1)} %param.11) | data formatting | bytes 4194304 | tf_op args[1]
  12.0 2.7 %all-to-all-done.1 = bf16[8,16,128]{2,0,1:T(8,128)(2,1)S(1)} async-done(((bf16[8,16,128]{2,0,1:T(8,128)(2,1)}), bf16[8,16,128]{2,0,1:T(8,128)(2,1)S(1)}, u32[]{:S(2)}, u32[]{:S(2)}) %all-to-all-start.1) | async-done | bytes 32800 | tf_op jit(solution)/shard_map/all_to_all | solution.py:75
  14.7 4.6 %all-to-all-start = ((bf16[512,16,128]{0,2,1:T(8,128)(2,1)}), bf16[512,16,128]{0,2,1:T(8,128)(2,1)}, u32[]{:S(2)}, u32[]{:S(2)}) async-start(bf16[512,16,128]{0,2,1:T(8,128)(2,1)} %bitcast.13), calls=%async_computation | async-start | bytes 4194304 | tf_op jit(solution)/shard_map/all_to_all | solution.py:73
  19.3 56.4 %all_gather.6 = bf16[128,2048]{1,0:T(8,128)(2,1)S(1)} all-gather(bf16[8,2048]{1,0:T(8,128)(2,1)S(1)} %copy-done.1), channel_id=1, replica_groups=mesh['groups'=2,'seq'=16] {'seq'}, dimensions={0}, use_global_device_ids=true | all-gather | bytes 557056 | tf_op jit(solution)/shard_map/all_gather | solution.py:66
  76.0 25.5 %all_gather.7 = bf16[128,2048]{1,0:T(8,128)(2,1)} all-gather(bf16[8,2048]{1,0:T(8,128)(2,1)S(1)} %copy-done.2), channel_id=1, replica_groups=mesh['groups'=2,'seq'=16] {'seq'}, dimensions={0}, use_global_device_ids=true | all-gather | bytes 557056 | tf_op jit(solution)/shard_map/all_gather | solution.py:67
  101.5 1.3 copy.53
  102.9 2.6 copy.59
  105.4 4.5 %all-to-all-start.2 = ((bf16[512,16,128]{0,2,1:T(8,128)(2,1)}), bf16[512,16,128]{0,2,1:T(8,128)(2,1)}, u32[]{:S(2)}, u32[]{:S(2)}) async-start(bf16[512,16,128]{0,2,1:T(8,128)(2,1)} %bitcast.19), calls=%async_computation.2 | async-start | bytes 4194304 | tf_op jit(solution)/shard_map/all_to_all | solution.py:74
  109.9 122.1 %while.29 = (s32[]{:T(128)}, f32[4,128,32]{1,0,2:T(4,128)S(1)}, f32[4,128,32]{1,0,2:T(4,128)S(1)}, f32[4,128,2048]{1,0,2:T(4,128)}, bf16[4,128,2048]{2,1,0:T(8,1...) while((s32[]{:T(128)}, f32[4,128,32]{1,0,2:T(4,128)S(1)}, ...), condition=%wide.region_3.4_spmd, body=%wide.region_0.3_spmd.sunk | while | flops 138403840 | bytes 13238389 | solution.py:49
  109.9 1.1 constant_dynamic-slice_fusion.5
  112.9 27.5 %dynamic_update_slice.16 = f32[4,128,2048]{1,0,2:T(4,128)} dynamic-update-slice(f32[4,128,2048]{1,0,2:T(4,128)} %get-tuple-element.322, f32[1,128,2048]{1,0,2:T(1,128)S(1)} %bitcast.142, s32[]{:T(128)S(6)} %copy.101, s32[]{:T(128)} %constant.28.clone.1..sunk, s32[]{:T(128)} %constant.28.clone.1..sunk) | dynamic-update-slice | bytes 2097156 | tf_op jit(solution)/shard_map/while/body/jit(dynamic_update_index_in_dim)/dynamic_update_slice | solution.py:49
  143.4 27.5 %dynamic_update_slice.16 = f32[4,128,2048]{1,0,2:T(4,128)} dynamic-update-slice(f32[4,128,2048]{1,0,2:T(4,128)} %get-tuple-element.322, f32[1,128,2048]{1,0,2:T(1,128)S(1)} %bitcast.142, s32[]{:T(128)S(6)} %copy.101, s32[]{:T(128)} %constant.28.clone.1..sunk, s32[]{:T(128)} %constant.28.clone.1..sunk) | dynamic-update-slice | bytes 2097156 | tf_op jit(solution)/shard_map/while/body/jit(dynamic_update_index_in_dim)/dynamic_update_slice | solution.py:49
  173.9 27.5 %dynamic_update_slice.16 = f32[4,128,2048]{1,0,2:T(4,128)} dynamic-update-slice(f32[4,128,2048]{1,0,2:T(4,128)} %get-tuple-element.322, f32[1,128,2048]{1,0,2:T(1,128)S(1)} %bitcast.142, s32[]{:T(128)S(6)} %copy.101, s32[]{:T(128)} %constant.28.clone.1..sunk, s32[]{:T(128)} %constant.28.clone.1..sunk) | dynamic-update-slice | bytes 2097156 | tf_op jit(solution)/shard_map/while/body/jit(dynamic_update_index_in_dim)/dynamic_update_slice | solution.py:49
  204.4 27.5 %dynamic_update_slice.16 = f32[4,128,2048]{1,0,2:T(4,128)} dynamic-update-slice(f32[4,128,2048]{1,0,2:T(4,128)} %get-tuple-element.322, f32[1,128,2048]{1,0,2:T(1,128)S(1)} %bitcast.142, s32[]{:T(128)S(6)} %copy.101, s32[]{:T(128)} %constant.28.clone.1..sunk, s32[]{:T(128)} %constant.28.clone.1..sunk) | dynamic-update-slice | bytes 2097156 | tf_op jit(solution)/shard_map/while/body/jit(dynamic_update_index_in_dim)/dynamic_update_slice | solution.py:49
  232.1 3.9 %copy.58 = bf16[16,512,128]{2,1,0:T(8,128)(2,1)} copy(bf16[16,512,128]{1,2,0:T(8,128)(2,1)} %bitcast.14) | data formatting | bytes 4194304 | tf_op jit(solution)/shard_map/all_to_all | solution.py:73
  236.0 3.9 %copy.60 = bf16[16,512,128]{2,1,0:T(8,128)(2,1)} copy(bf16[16,512,128]{1,2,0:T(8,128)(2,1)} %bitcast.20) | data formatting | bytes 4194304 | tf_op jit(solution)/shard_map/all_to_all | solution.py:74
  239.9 10.5 %while.30 = (s32[]{:T(128)}, f32[128,2]{0,1:T(2,128)S(1)}, f32[128,2]{0,1:T(2,128)S(1)}, f32[128,128]{0,1:T(8,128)S(1)}, bf16[2,4096,128]{2,1,0:T(8,128)(2,1)}, ...) while((s32[]{:T(128)}, f32[128,2]{0,1:T(2,128)S(1)}, ...), condition=%wide.region_7.8_spmd.clone, body=%wide.region_4.7_spmd.clone.sunk | while | flops 274793984 | bytes 23378036 | solution.py:85
  239.9 1.7 constant_dynamic-slice_fusion.6
  245.2 1.7 constant_dynamic-slice_fusion.6
  251.2 5.9 %all-to-all-start.3 = ((bf16[16,8,128]{2,1,0:T(8,128)(2,1)}), bf16[16,8,128]{2,1,0:T(8,128)(2,1)S(1)}, u32[]{:S(2)}, u32[]{:S(2)}) async-start(bf16[16,8,128]{2,1,0:T(8,128)(2,1)} %bitcast.23), calls=%async_computation.3 | async-start | bytes 65536 | tf_op jit(solution)/shard_map/all_to_all | solution.py:94
  257.1 2.9 %fusion.23 = bf16[512,2048]{0,1:T(8,128)(2,1)S(1)} fusion(f32[256,8,4,128]{3,2,1,0:T(4,128)} %bitcast.150, f32[512,32]{0,1:T(8,128)S(1)} %get-tuple-element.202, f32[512,32]{0,1:T(8,128)S(1)} %get-tuple-element.203, f32[512,32]{0,1:T(8,128)S(1)} %get-tuple-element.201), kind=kLoop, calls=%fused_computation.33 | loop fusion | flops 4194304 | bytes 6488064 | tf_op jit(solution)/shard_map/convert_element_type | solution.py:71
  260.0 2.4 copy.65
  262.4 1.3 all-to-all-done.3
  (61 shorter events, 19.6 us)
Async XLA Ops:
  0.6 14.0 %all-to-all-start.1 = ((bf16[8,16,128]{2,0,1:T(8,128)(2,1)}), bf16[8,16,128]{2,0,1:T(8,128)(2,1)S(1)}, u32[]{:S(2)}, u32[]{:S(2)}) async-start(bf16[8,16,128]{2,0,1:T(8,128)(2,1)} %bitcast.158), calls=%async_computation.1 | async-start | bytes 65536 | tf_op jit(solution)/shard_map/all_to_all | solution.py:75
  14.7 4.6 %copy-start.1 = (bf16[8,2048]{1,0:T(8,128)(2,1)S(1)}, bf16[8,2048]{1,0:T(8,128)(2,1)}, u32[]{:S(2)}) copy-start(bf16[8,2048]{1,0:T(8,128)(2,1)} %param.14) | copy-start | bytes 98308
  14.7 61.4 %copy-start.2 = (bf16[8,2048]{1,0:T(8,128)(2,1)S(1)}, bf16[8,2048]{1,0:T(8,128)(2,1)}, u32[]{:S(2)}) copy-start(bf16[8,2048]{1,0:T(8,128)(2,1)} %param.15) | copy-start | bytes 98308
  14.7 90.8 %all-to-all-start = ((bf16[512,16,128]{0,2,1:T(8,128)(2,1)}), bf16[512,16,128]{0,2,1:T(8,128)(2,1)}, u32[]{:S(2)}, u32[]{:S(2)}) async-start(bf16[512,16,128]{0,2,1:T(8,128)(2,1)} %bitcast.13), calls=%async_computation | async-start | bytes 4194304 | tf_op jit(solution)/shard_map/all_to_all | solution.py:73
  19.2 83.6 %copy-start = (bf16[512,2048]{1,0:T(8,128)(2,1)S(1)}, bf16[512,2048]{1,0:T(8,128)(2,1)}, u32[]{:S(2)}) copy-start(bf16[512,2048]{1,0:T(8,128)(2,1)} %param.12) | copy-start | bytes 6291460
  105.4 130.6 %all-to-all-start.2 = ((bf16[512,16,128]{0,2,1:T(8,128)(2,1)}), bf16[512,16,128]{0,2,1:T(8,128)(2,1)}, u32[]{:S(2)}, u32[]{:S(2)}) async-start(bf16[512,16,128]{0,2,1:T(8,128)(2,1)} %bitcast.19), calls=%async_computation.2 | async-start | bytes 4194304 | tf_op jit(solution)/shard_map/all_to_all | solution.py:74
  251.2 12.5 %all-to-all-start.3 = ((bf16[16,8,128]{2,1,0:T(8,128)(2,1)}), bf16[16,8,128]{2,1,0:T(8,128)(2,1)S(1)}, u32[]{:S(2)}, u32[]{:S(2)}) async-start(bf16[16,8,128]{2,1,0:T(8,128)(2,1)} %bitcast.23), calls=%async_computation.3 | async-start | bytes 65536 | tf_op jit(solution)/shard_map/all_to_all | solution.py:94
where the time goes:
time: 268 us; the launch traced here: 264 us
  local copies, waits for them, and re-layouts  142 us (53%)
  blocking collectives  81.9 us (31%)
  starting transfers between devices  22.3 us (8%)
  matrix products  7.69 us (3%)
  other arithmetic  5.8 us (2%)
  waiting for transfers between devices  4.06 us (2%)
    dynamic_update_slice x12, local copies, waits for them, and re-layouts, blocked_partial(): lax.map(lambda query_rows: partial_block(query_rows, keys, values), stacked)  111 us
    all_gather x1, blocking collectives, local(): lax.all_gather(audio_k, 'seq', axis=0, tiled=True)  56.4 us
    all_gather x1, blocking collectives, local(): lax.all_gather(audio_v, 'seq', axis=0, tiled=True)  25.5 us
    unnamed x11, local copies, waits for them, and re-layouts  9.6 us
    all_to_all x1, starting transfers between devices, local(): lax.all_to_all(audio_q, 'seq', split_axis=1, concat_axis=0, tiled=True)  7.4 us
    all_to_all x1, starting transfers between devices, local(): lax.all_to_all(head_out, 'seq', split_axis=0, concat_axis=1, tiled=True)  5.89 us
    dynamic_slice x6, local copies, waits for them, and re-layouts, local(): lax.scan(advance, empty_state(query_heads.shape[0], columns), (key_heads....  5.49 us
    dynamic_slice x8, local copies, waits for them, and re-layouts, blocked_partial(): lax.map(lambda query_rows: partial_block(query_rows, keys, values), stacked)  5.4 us
  transfers between devices with their start and end apart: 4, of which 2 were waited for; matrix products, arithmetic and copies ran while one was open for 53% of the time, Pallas kernels for 0%

commit v1 on v0

--- a/solution.py
+++ b/solution.py
@@ -71,7 +71,12 @@
     video_out = (summed / spread(totals)).astype(jnp.bfloat16)
     key_heads, value_heads, query_heads = (
         lax.all_to_all(video_k, "seq", split_axis=1, concat_axis=0, tiled=True),
-        lax.all_to_all(video_v, "seq", split_axis=1, concat_axis=0, tiled=True),
+        jnp.concatenate(
+            lax.all_to_all(
+                jnp.stack(jnp.split(video_v, lax.axis_size("seq"), axis=1)), "seq", 0, 0
+            ),
+            axis=0,
+        ),
         lax.all_to_all(audio_q, "seq", split_axis=1, concat_axis=0, tiled=True),
     )
     total_keys = key_heads.shape[0]

time: 268 us -> 298 us (1.11)
  local copies, waits for them, and re-layouts: 142 us -> 166 us
  matrix products: 7.69 us -> 16 us
    all_gather x1, blocking collectives: 56.4 us -> 23.5 us  [local(): lax.all_gather(audio_k, 'seq', axis=0, tiled=True)]
    all_gather x1, blocking collectives: 25.5 us -> 56.6 us  [local(): lax.all_gather(audio_v, 'seq', axis=0, tiled=True)]
    unnamed x11 -> x23, local copies, waits for them, and re-layouts: 9.6 us -> 31.7 us
    dot_general x6, matrix products: 3.77 us -> 7.94 us  [partial_block(): jnp.einsum('hrs,shd->rhd', weights.astype(jnp.bfloat16), value_heads, pre...]
    dot_general x6, matrix products: 3.92 us -> 8.09 us  [partial_block(): jnp.einsum('rhd,shd->hrs', query_heads, key_heads, preferred_element_type...]
    all_to_all x1 -> x0, local copies, waits for them, and re-layouts: 3.91 us -> none  [local(): lax.all_to_all(video_v, 'seq', split_axis=1, concat_axis=0, tiled=True)]
    while x0 -> x8, local copies, waits for them, and re-layouts: none -> 3.89 us
  transfers between devices with their start and end apart: 4 -> 4, of which waited for: 2 -> 1; matrix products, arithmetic and copies ran while one was open for 53% -> 58% of each run, Pallas kernels for 0% -> 0%
where the time goes in v1:
time: 298 us; the launch traced here: 294 us
  local copies, waits for them, and re-layouts  166 us (56%)
  blocking collectives  80 us (27%)
  starting transfers between devices  24.2 us (8%)
  matrix products  16 us (5%)
  other arithmetic  5.8 us (2%)
    dynamic_update_slice x12, local copies, waits for them, and re-layouts, blocked_partial(): lax.map(lambda query_rows: partial_block(query_rows, keys, values), stacked)  111 us
    all_gather x1, blocking collectives, local(): lax.all_gather(audio_v, 'seq', axis=0, tiled=True)  56.6 us
    unnamed x23, local copies, waits for them, and re-layouts  31.7 us
    all_gather x1, blocking collectives, local(): lax.all_gather(audio_k, 'seq', axis=0, tiled=True)  23.5 us
    dot_general x6, matrix products, partial_block(): jnp.einsum('rhd,shd->hrs', query_heads, key_heads, preferred_element_type...  8.09 us
    dot_general x6, matrix products, partial_block(): jnp.einsum('hrs,shd->rhd', weights.astype(jnp.bfloat16), value_heads, pre...  7.94 us
    all_to_all x1, starting transfers between devices, local(): lax.all_to_all(audio_q, 'seq', split_axis=1, concat_axis=0, tiled=True)  7.4 us
    all_to_all x1, starting transfers between devices, local(): lax.all_to_all(jnp.stack(jnp.split(video_v, lax.axis_size('seq'), axis=1)...  6.94 us
  transfers between devices with their start and end apart: 4, of which 1 were waited for; matrix products, arithmetic and copies ran while one was open for 58% of the time, Pallas kernels for 0%

profile of v1, /device:TPU:0, one launch (start us, length us, event | category | flops | bytes accessed | tf_op | source)
XLA Modules:
  0.0 293.9 jit_solution(12636935950401744175)
XLA Ops:
  0.6 7.4 %all-to-all-start.1 = ((bf16[8,16,128]{2,0,1:T(8,128)(2,1)}), bf16[8,16,128]{2,0,1:T(8,128)(2,1)S(1)}, u32[]{:S(2)}, u32[]{:S(2)}) async-start(bf16[8,16,128]{2,0,1:T(8,128)(2,1)} %bitcast.188), calls=%async_computation.1 | async-start | bytes 65536 | tf_op jit(solution)/shard_map/all_to_all | solution.py:80
  8.0 23.5 %all_gather.6 = bf16[128,2048]{1,0:T(8,128)(2,1)S(1)} all-gather(bf16[8,2048]{1,0:T(8,128)(2,1)} %param.14), channel_id=1, replica_groups=mesh['groups'=2,'seq'=16] {'seq'}, dimensions={0}, use_global_device_ids=true | all-gather | bytes 557056 | tf_op jit(solution)/shard_map/all_gather | solution.py:66
  32.5 3.9 %copy.55 = bf16[512,2048]{0,1:T(8,128)(2,1)} copy(bf16[512,2048]{1,0:T(8,128)(2,1)} %param.11) | data formatting | bytes 4194304 | tf_op args[1]
  36.4 3.9 %all-to-all-start = ((bf16[512,16,128]{0,2,1:T(8,128)(2,1)}), bf16[512,16,128]{0,2,1:T(8,128)(2,1)S(1)}, u32[]{:S(2)}, u32[]{:S(2)}) async-start(bf16[512,16,128]{0,2,1:T(8,128)(2,1)} %bitcast.178), calls=%async_computation | async-start | bytes 4194304 | tf_op jit(solution)/shard_map/all_to_all | solution.py:73
  40.3 56.6 %all_gather.7 = bf16[128,2048]{1,0:T(8,128)(2,1)S(1)} all-gather(bf16[8,2048]{1,0:T(8,128)(2,1)S(1)} %copy-done.3), channel_id=1, replica_groups=mesh['groups'=2,'seq'=16] {'seq'}, dimensions={0}, use_global_device_ids=true | all-gather | bytes 557056 | tf_op jit(solution)/shard_map/all_gather | solution.py:67
  97.9 1.6 bitcast_dynamic-update-slice_fusion.15
  101.0 1.6 bitcast_dynamic-update-slice_fusion.13
  104.1 1.6 bitcast_dynamic-update-slice_fusion.11
  107.2 1.6 bitcast_dynamic-update-slice_fusion.9
  119.7 1.6 bitcast_dynamic-update-slice_fusion.1
  121.3 1.6 bitcast_dynamic-update-slice_fusion
  124.1 6.9 %all-to-all-start.2 = ((bf16[16,512,128]{2,1,0:T(8,128)(2,1)}), bf16[16,512,128]{2,1,0:T(8,128)(2,1)S(1)}, u32[]{:S(2)}, u32[]{:S(2)}) async-start(bf16[16,512,128]{2,1,0:T(8,128)(2,1)} %bitcast_dynamic-update-slice_fusion), calls=%async_computation.2 | async-start | bytes 4194304 | tf_op jit(solution)/shard_map/all_to_all | solution.py:75
  131.1 130.4 %while.29 = (s32[]{:T(128)}, f32[4,128,32]{1,0,2:T(4,128)S(1)}, f32[4,128,32]{1,0,2:T(4,128)S(1)}, f32[4,128,2048]{1,0,2:T(4,128)}, bf16[4,128,2048]{2,1,0:T(8,1...) while((s32[]{:T(128)}, f32[4,128,32]{1,0,2:T(4,128)S(1)}, ...), condition=%wide.region_3.4_spmd, body=%wide.region_0.3_spmd.sunk | while | flops 138403840 | bytes 13238389 | solution.py:49
  136.2 27.5 %dynamic_update_slice.16 = f32[4,128,2048]{1,0,2:T(4,128)} dynamic-update-slice(f32[4,128,2048]{1,0,2:T(4,128)} %get-tuple-element.322, f32[1,128,2048]{1,0,2:T(1,128)S(1)} %bitcast.172, s32[]{:T(128)S(6)} %copy.97, s32[]{:T(128)} %constant.28.clone.1..sunk, s32[]{:T(128)} %constant.28.clone.1..sunk) | dynamic-update-slice | bytes 2097156 | tf_op jit(solution)/shard_map/while/body/jit(dynamic_update_index_in_dim)/dynamic_update_slice | solution.py:49
  168.7 27.5 %dynamic_update_slice.16 = f32[4,128,2048]{1,0,2:T(4,128)} dynamic-update-slice(f32[4,128,2048]{1,0,2:T(4,128)} %get-tuple-element.322, f32[1,128,2048]{1,0,2:T(1,128)S(1)} %bitcast.172, s32[]{:T(128)S(6)} %copy.97, s32[]{:T(128)} %constant.28.clone.1..sunk, s32[]{:T(128)} %constant.28.clone.1..sunk) | dynamic-update-slice | bytes 2097156 | tf_op jit(solution)/shard_map/while/body/jit(dynamic_update_index_in_dim)/dynamic_update_slice | solution.py:49
  201.3 27.5 %dynamic_update_slice.16 = f32[4,128,2048]{1,0,2:T(4,128)} dynamic-update-slice(f32[4,128,2048]{1,0,2:T(4,128)} %get-tuple-element.322, f32[1,128,2048]{1,0,2:T(1,128)S(1)} %bitcast.172, s32[]{:T(128)S(6)} %copy.97, s32[]{:T(128)} %constant.28.clone.1..sunk, s32[]{:T(128)} %constant.28.clone.1..sunk) | dynamic-update-slice | bytes 2097156 | tf_op jit(solution)/shard_map/while/body/jit(dynamic_update_index_in_dim)/dynamic_update_slice | solution.py:49
  233.9 27.5 %dynamic_update_slice.16 = f32[4,128,2048]{1,0,2:T(4,128)} dynamic-update-slice(f32[4,128,2048]{1,0,2:T(4,128)} %get-tuple-element.322, f32[1,128,2048]{1,0,2:T(1,128)S(1)} %bitcast.172, s32[]{:T(128)S(6)} %copy.97, s32[]{:T(128)} %constant.28.clone.1..sunk, s32[]{:T(128)} %constant.28.clone.1..sunk) | dynamic-update-slice | bytes 2097156 | tf_op jit(solution)/shard_map/while/body/jit(dynamic_update_index_in_dim)/dynamic_update_slice | solution.py:49
  261.6 3.9 %copy.56 = bf16[16,512,128]{2,1,0:T(8,128)(2,1)} copy(bf16[16,512,128]{1,2,0:T(8,128)(2,1)} %bitcast.177) | data formatting | bytes 4194304 | tf_op jit(solution)/shard_map/all_to_all | solution.py:73
  265.5 14.4 %while.30 = (s32[]{:T(128)}, f32[128,2]{0,1:T(2,128)S(1)}, f32[128,2]{0,1:T(2,128)S(1)}, f32[128,128]{0,1:T(8,128)S(1)}, bf16[2,4096,128]{2,1,0:T(8,128)(2,1)}, ...) while((s32[]{:T(128)}, f32[128,2]{0,1:T(2,128)S(1)}, ...), condition=%wide.region_7.8_spmd.clone, body=%wide.region_4.7_spmd.clone.sunk | while | flops 274793984 | bytes 40155304 | solution.py:90
  266.8 1.7 constant_dynamic-slice_fusion.6
  274.0 1.7 constant_dynamic-slice_fusion.6
  280.6 6.0 %all-to-all-start.3 = ((bf16[16,8,128]{2,1,0:T(8,128)(2,1)}), bf16[16,8,128]{2,1,0:T(8,128)(2,1)S(1)}, u32[]{:S(2)}, u32[]{:S(2)}) async-start(bf16[16,8,128]{2,1,0:T(8,128)(2,1)} %bitcast.37), calls=%async_computation.3 | async-start | bytes 65536 | tf_op jit(solution)/shard_map/all_to_all | solution.py:99
  286.7 2.9 fusion.23
  289.5 2.4 copy.61
  (81 shorter events, 52.8 us)
Async XLA Ops:
  0.6 35.8 %all-to-all-start.1 = ((bf16[8,16,128]{2,0,1:T(8,128)(2,1)}), bf16[8,16,128]{2,0,1:T(8,128)(2,1)S(1)}, u32[]{:S(2)}, u32[]{:S(2)}) async-start(bf16[8,16,128]{2,0,1:T(8,128)(2,1)} %bitcast.188), calls=%async_computation.1 | async-start | bytes 65536 | tf_op jit(solution)/shard_map/all_to_all | solution.py:80
  36.4 3.9 %copy-start.3 = (bf16[8,2048]{1,0:T(8,128)(2,1)S(1)}, bf16[8,2048]{1,0:T(8,128)(2,1)}, u32[]{:S(2)}) copy-start(bf16[8,2048]{1,0:T(8,128)(2,1)} %param.15) | copy-start | bytes 98308
  36.4 86.4 %all-to-all-start = ((bf16[512,16,128]{0,2,1:T(8,128)(2,1)}), bf16[512,16,128]{0,2,1:T(8,128)(2,1)S(1)}, u32[]{:S(2)}, u32[]{:S(2)}) async-start(bf16[512,16,128]{0,2,1:T(8,128)(2,1)} %bitcast.178), calls=%async_computation | async-start | bytes 4194304 | tf_op jit(solution)/shard_map/all_to_all | solution.py:73
  122.8 1.3 copy-start.2
  124.1 141.3 %all-to-all-start.2 = ((bf16[16,512,128]{2,1,0:T(8,128)(2,1)}), bf16[16,512,128]{2,1,0:T(8,128)(2,1)S(1)}, u32[]{:S(2)}, u32[]{:S(2)}) async-start(bf16[16,512,128]{2,1,0:T(8,128)(2,1)} %bitcast_dynamic-update-slice_fusion), calls=%async_computation.2 | async-start | bytes 4194304 | tf_op jit(solution)/shard_map/all_to_all | solution.py:75
  265.5 1.3 copy-start
  271.1 1.6 copy-start.1
  272.7 1.3 copy-start
  278.3 1.6 copy-start.1
  280.6 12.6 %all-to-all-start.3 = ((bf16[16,8,128]{2,1,0:T(8,128)(2,1)}), bf16[16,8,128]{2,1,0:T(8,128)(2,1)S(1)}, u32[]{:S(2)}, u32[]{:S(2)}) async-start(bf16[16,8,128]{2,1,0:T(8,128)(2,1)} %bitcast.37), calls=%async_computation.3 | async-start | bytes 65536 | tf_op jit(solution)/shard_map/all_to_all | solution.py:99
